TPU v7x, 32 devices: a whole 2x2x4 slice. The times are simulated.
32 devices in a mesh: groups: 2 (over y), picks: 4 (over z), heads: 4 (over x, core).
Axes of the slice: x: 2, y: 2, z: 4, core: 2. Of those that a mesh axis runs over, the one named last changes fastest.
Arguments:
- coords: float32 [3, 8192], P(None, ('groups', 'picks')), parts along dimension 1, may hold values from -1 to 1
- horizon_ids: int32 [8192], P(('groups', 'picks')), parts along dimension 0, may hold values from 0 to 63
- horizon_levels: float32 [128], P('groups'), parts along dimension 0, may hold values from -2 to 2
- latents: bfloat16 [512, 1024], replicated, may hold values from -960 to 960
- kv_weight: bfloat16 [3072, 2, 1024], P('picks', None, 'heads'), may hold values from -0.109375 to 0.109375
- cross_out: bfloat16 [1024, 1024], P('heads'), may hold values from -0.75 to 0.75
- norm_gains: float32 [2, 1024], replicated, may hold values from 0.1 to 1.9
- self_qkv: bfloat16 [3, 1024, 1024], P(None, None, 'heads'), may hold values from -0.1875 to 0.1875
- self_out: bfloat16 [1024, 1024], P(None, 'heads'), may hold values from -0.1875 to 0.1875
- dec_kv: bfloat16 [2, 1024, 1024], P(None, None, 'heads'), may hold values from -0.1875 to 0.1875
- dec_query: bfloat16 [3072, 1024], P('picks', 'heads'), may hold values from -0.109375 to 0.109375
- readout: float32 [1024], P('heads'), may hold values from -0.1875 to 0.1875
Outputs:
- field: float32 [8192], P(('groups', 'picks')), parts along dimension 0
- latents_out: float32 [1024, 1024], P('groups', 'heads'), parts along dimension 0
- grad_query: float32 [6144, 1024], P(('groups', 'picks'), 'heads'), parts along dimension 0
There are 2 independent parts, one for each index of `groups`. A program takes and returns all parts, laid end to end along the dimension named above; an argument that names none is the same for every part. Nothing has to cross between parts.
All inputs are finite; a program needn't handle non-finite values.
Results may differ from a plain program's by a relative error of at most 0.028.
Values may be sent and summed in bfloat16 or wider, within the bound.
No kernel may reach another device: no remote copies, remote signals or barrier semaphores. Data moves between devices by JAX's collectives and lax.ppermute only.
A program may use at most 64 MiB of HBM per device.

v0:
```python
import functools
import jax
import jax.numpy as jnp
from jax import lax
from jax.sharding import PartitionSpec as P

HEAD = 128
BANDS = 512
HORIZONS = 64
PI = 3.141592653589793
EPS = 1e-06
RING_MAX = 4


def encode(coords):
    freq = jnp.linspace(1.0, BANDS / 2.0, BANDS).astype(jnp.float32)
    angle = PI * freq[None, :, None] * coords[:, None, :]
    table = jnp.concatenate([jnp.sin(angle), jnp.cos(angle)], axis=0)
    return table.reshape(6 * BANDS, coords.shape[1]).T.astype(jnp.bfloat16)


def ring_gather(x, axis, n):
    if n == 1:
        return x
    if n > RING_MAX:
        return lax.all_gather(x, axis, axis=0, tiled=True)
    idx = lax.axis_index(axis)
    blocks = [x]
    for s in range(1, n):
        blocks.append(lax.ppermute(x, axis, [(i, (i - s) % n) for i in range(n)]))
    flipped = jnp.stack(blocks)
    ordered = jnp.roll(flipped, idx, axis=0)
    return ordered.reshape((n * x.shape[0],) + x.shape[1:])


def fetch_rows(kv_weight, n_picks, n_groups):
    if n_groups != 2:
        return lax.all_gather(kv_weight, "picks", axis=0, tiled=True)
    g = lax.axis_index("groups")
    rows = kv_weight.shape[0] // 2
    mine = lax.dynamic_slice_in_dim(kv_weight, g * rows, rows, 0)
    first = max(8, 2 * rows // 3 // 8 * 8)
    bounds = [(0, first), (first, rows)] if first < rows else [(0, rows)]
    own, other = ([], [])
    for lo, hi in bounds:
        gathered = lax.all_gather(mine[lo:hi], "picks", axis=0, tiled=False)
        own.append(gathered)
        other.append(lax.ppermute(gathered, "groups", [(0, 1), (1, 0)]))
    halves = jnp.stack([jnp.concatenate(own, axis=1), jnp.concatenate(other, axis=1)], axis=1)
    halves = jnp.roll(halves, g, axis=1)
    return halves.reshape((n_picks * kv_weight.shape[0],) + kv_weight.shape[1:])


def pair_sum(x, axis, n):
    if n != 4:
        return lax.psum(x, axis)
    x = x + lax.ppermute(x, axis, [(k, k ^ 1) for k in range(n)])
    return x + lax.ppermute(x, axis, [(k, k ^ 2) for k in range(n)])


def on_device(
    coords,
    horizon_ids,
    horizon_levels,
    latents,
    kv_weight,
    cross_out,
    norm_gains,
    self_qkv,
    self_out,
    dec_kv,
    dec_query,
    readout,
    *,
    n_picks,
    n_heads,
    n_groups
):
    high = lax.Precision.HIGHEST
    scale = HEAD ** (-0.5)
    count = coords.shape[1]
    width = latents.shape[1]
    lat_rows = latents.shape[0]
    local = kv_weight.shape[2]
    nheads = local // HEAD
    column = lax.axis_index("heads") * local
    enc = encode(coords)
    cross_full = ring_gather(cross_out, "heads", n_heads)
    piece = lax.all_gather(kv_weight, "picks", axis=0, tiled=True)
    cross_full, piece = lax.optimization_barrier((cross_full, piece))
    keys_vals = jnp.einsum("tf,fjc->tjc", enc, piece, preferred_element_type=jnp.float32).astype(
        jnp.bfloat16
    )
    keys = keys_vals[:, 0].reshape(count, nheads, HEAD)
    values = keys_vals[:, 1].reshape(count, nheads, HEAD)
    queries = lax.dynamic_slice_in_dim(latents, column, local, 1).reshape(lat_rows, nheads, HEAD)
    scores = jnp.einsum("lhc,thc->hlt", queries, keys, preferred_element_type=jnp.float32) * scale
    top = jnp.max(scores, axis=2)
    expo = jnp.exp(scores - top[:, :, None])
    total = jnp.sum(expo, axis=2)
    numer = jnp.einsum(
        "hlt,thc->hlc", expo.astype(jnp.bfloat16), values, preferred_element_type=jnp.float32
    )
    all_numer = lax.all_gather(numer.astype(jnp.bfloat16), "picks", axis=0, tiled=False)
    all_stats = lax.all_gather(jnp.stack([top, total]), "picks", axis=0, tiled=False)
    best = jnp.max(all_stats[:, 0], axis=0)
    factor = jnp.exp(all_stats[:, 0] - best[None])
    merged_total = jnp.sum(factor * all_stats[:, 1], axis=0)
    merged_numer = jnp.einsum(
        "phl,phlc->hlc", factor, all_numer.astype(jnp.float32), precision=high
    )
    attended = (
        (merged_numer / merged_total[:, :, None])
        .transpose(1, 0, 2)
        .reshape(lat_rows, local)
        .astype(jnp.bfloat16)
    )
    out_full = ring_gather(self_out.T, "heads", n_heads).T
    out_full, attended = lax.optimization_barrier((out_full, attended))
    dq_local, attended = lax.optimization_barrier((dec_query, attended))
    dq_full = lax.all_gather(dq_local, "picks", axis=0, tiled=True)
    attended_full = ring_gather(attended.T, "heads", n_heads).T
    whole = latents.astype(jnp.float32) + jnp.dot(
        attended_full, cross_full, preferred_element_type=jnp.float32
    )
    power = jnp.mean(whole * whole, axis=1, keepdims=True)
    normed = (whole * lax.rsqrt(power + EPS) * norm_gains[0][None, :]).astype(jnp.bfloat16)
    state = lax.dynamic_slice_in_dim(whole, column, local, 1)
    qkv = jnp.einsum("ld,kde->kle", normed, self_qkv, preferred_element_type=jnp.float32).astype(
        jnp.bfloat16
    )
    self_q = qkv[0].reshape(lat_rows, nheads, HEAD)
    self_k = qkv[1].reshape(lat_rows, nheads, HEAD)
    self_v = qkv[2].reshape(lat_rows, nheads, HEAD)
    inner = jnp.einsum("lhc,mhc->hlm", self_q, self_k, preferred_element_type=jnp.float32) * scale
    raised = jnp.exp(inner)
    probs = (raised / jnp.sum(raised, axis=2, keepdims=True)).astype(jnp.bfloat16)
    head_out = (
        jnp.einsum("hlm,mhc->lhc", probs, self_v, preferred_element_type=jnp.float32)
        .astype(jnp.bfloat16)
        .reshape(lat_rows, local)
    )
    every_head = ring_gather(head_out.T, "heads", n_heads).T
    out_whole = whole + jnp.dot(every_head, out_full, preferred_element_type=jnp.float32)
    latents_out = lax.dynamic_slice_in_dim(out_whole, column, local, 1)
    power_two = jnp.mean(out_whole * out_whole, axis=1, keepdims=True)
    normed2 = (out_whole * lax.rsqrt(power_two + EPS) * norm_gains[1][None, :]).astype(jnp.bfloat16)
    dec = jnp.einsum("ld,kde->kle", normed2, dec_kv, preferred_element_type=jnp.float32).astype(
        jnp.bfloat16
    )
    dec_keys = dec[0].reshape(lat_rows, nheads, HEAD)
    dec_vals = dec[1].reshape(lat_rows, nheads, HEAD)
    query = jnp.dot(enc, dq_full, preferred_element_type=jnp.float32).astype(jnp.bfloat16)
    dec_q = query.reshape(count, nheads, HEAD)
    logits = jnp.einsum("thc,lhc->htl", dec_q, dec_keys, preferred_element_type=jnp.float32) * scale
    lifted = jnp.exp(logits)
    weights = lifted / jnp.sum(lifted, axis=2, keepdims=True)
    out = jnp.einsum(
        "htl,lhc->thc", weights.astype(jnp.bfloat16), dec_vals, preferred_element_type=jnp.float32
    )
    read = readout.reshape(nheads, HEAD)
    onehot = (horizon_ids[:, None] == jnp.arange(HORIZONS, dtype=jnp.int32)[None, :]).astype(
        jnp.float32
    )
    target = jnp.sum(onehot * horizon_levels[None, :], axis=1)
    value_read = jnp.einsum("lhc,hc->hl", dec_vals.astype(jnp.float32), read, precision=high)
    lever = (
        weights
        * (
            value_read[:, None, :]
            - jnp.sum(value_read[:, None, :] * weights, axis=2, keepdims=True)
        )
    ).astype(jnp.bfloat16)
    pull = jnp.einsum("htl,lhc->thc", lever, dec_keys, preferred_element_type=jnp.float32) * scale
    field = pair_sum(jnp.sum(out * read[None, :, :], axis=(1, 2)), "heads", n_heads)
    miss = field - target
    dquery = (miss[:, None, None] * pull).reshape(count, local).astype(jnp.bfloat16)
    grad_query = lax.psum_scatter(
        jnp.dot(enc.T, dquery, preferred_element_type=jnp.float32).astype(jnp.bfloat16),
        "picks",
        scatter_dimension=0,
        tiled=True,
    ).astype(jnp.float32)
    return (field, latents_out, grad_query)


def solution(mesh):
    in_specs = (
        P(None, ("groups", "picks")),
        P(("groups", "picks")),
        P("groups"),
        P(),
        P("picks", None, "heads"),
        P("heads", None),
        P(),
        P(None, None, "heads"),
        P(None, "heads"),
        P(None, None, "heads"),
        P("picks", "heads"),
        P("heads"),
    )
    out_specs = (P(("groups", "picks")), P("groups", "heads"), P(("groups", "picks"), "heads"))
    body = functools.partial(
        on_device,
        n_picks=mesh.shape["picks"],
        n_heads=mesh.shape["heads"],
        n_groups=mesh.shape["groups"],
    )
    return jax.shard_map(body, mesh=mesh, in_specs=in_specs, out_specs=out_specs, check_vma=False)
```

profile of v0, /device:TPU:0, one launch (start us, length us, event | category | flops | bytes accessed | tf_op | source)
XLA Modules:
  0.0 216.1 jit_solution(17237952158772773728)
XLA Ops:
  8.0 1.2 copy.60
  9.2 2.4 %collective-permute-start = (bf16[256,1024]{1,0:T(8,128)(2,1)S(1)}, bf16[256,1024]{1,0:T(8,128)(2,1)S(1)}, u32[]{:S(2)}, u32[]{:S(2)}) collective-permute-start(bf16[256,1024]{1,0:T(8,128)(2,1)S(1)} %bitcast.124), channel_id=1, source_target_pairs={{0,3},{1,0},{2,1},{3,2},{4,7},{5,4},{6,5},{7,6},{8,11},{9,8},{10,9... | collective-permute-start | bytes 1572872 | tf_op jit(solution)/shard_map/ppermute | solution.py:30
  12.4 1.7 collective-permute-start.4
  15.3 22.8 %fusion = (bf16[3,512,1024]{2,1,0:T(8,128)(2,1)S(1)}, bf16[3,512,1024]{2,1,0:T(8,128)(2,1)S(1)}) fusion(f32[3,1024]{1,0:T(4,128)S(1)} %copy-done.9, f32[512]{0:T(512)S(1)} %maximum_multiply_fusion), kind=kLoop, calls=%fused_computation.2 | loop fusion | flops 4718592 | bytes 6305792 | tf_op jit(solution)/shard_map/convert
  38.2 3.2 %pad_maximum_fusion = bf16[6,512,1024]{2,1,0:T(8,128)(2,1)} fusion(bf16[3,512,1024]{2,1,0:T(8,128)(2,1)S(1)} %get-tuple-element.29, bf16[3,512,1024]{2,1,0:T(8,128)(2,1)S(1)} %get-tuple-element.28), kind=kLoop, calls=%fused_computation.4 | loop fusion | flops 3145728 | bytes 12582912 | tf_op jit(solution)/shard_map/concatenate | solution.py:18
  41.4 5.1 %collective-permute-done.3 = bf16[256,1024]{1,0:T(8,128)(2,1)} collective-permute-done((bf16[256,1024]{1,0:T(8,128)(2,1)}, bf16[256,1024]{1,0:T(8,128)(2,1)}, u32[]{:S(2)}, u32[]{:S(2)}) %collective-permute-start.3) | collective-permute-done | bytes 524320 | tf_op jit(solution)/shard_map/ppermute | solution.py:30
  47.5 8.8 %collective-permute-done.4 = bf16[256,1024]{1,0:T(8,128)(2,1)} collective-permute-done((bf16[256,1024]{1,0:T(8,128)(2,1)}, bf16[256,1024]{1,0:T(8,128)(2,1)}, u32[]{:S(2)}, u32[]{:S(2)}) %collective-permute-start.4) | collective-permute-done | bytes 524320 | tf_op jit(solution)/shard_map/ppermute | solution.py:30
  56.3 5.1 %fusion.14 = bf16[4,256,1024]{2,1,0:T(8,128)(2,1)} fusion(s32[]{:T(128)S(6)} %select_n.27, bf16[1,256,1024]{2,1,0:T(8,128)(2,1)S(1)} %bitcast.143, bf16[1,256,1024]{2,1,0:T(8,128)(2,1)} %bitcast.13, bf16[1,256,1024]{2,1,0:T(8,128)(2,1)} %bitcast.14, bf16[1,256,1024]{2,1,0:T(8,128)(2,1)} %bitcast.15), kind=kLoop, calls=%fused_computation.38 | loop fusion | flops 7340032 | bytes 4194308 | tf_op jit(solution)/shard_map/jit(_roll_dynamic)/concatenate | solution.py:32
  61.4 14.5 %all-gather.6.cloned.1.call-done = bf16[3072,2,256]{2,1,0:T(2,128)(2,1)} async-done(((bf16[768,2,256]{2,1,0:T(2,128)(2,1)}), bf16[3072,2,256]{2,1,0:T(2,128)(2,1)}) %all-gather.6.cloned.1.call-update) | async-done | bytes 3145744 | tf_op jit(solution)/shard_map/all_gather | solution.py:89
  75.8 7.1 %fusion.32 = bf16[1024,2,256]{0,2,1:T(8,128)(2,1)S(1)} fusion(bf16[3072,1024,1]{1,0,2:T(8,128)(2,1)} %bitcast.118, bf16[3072,2,256]{2,1,0:T(2,128)(2,1)} %all-gather.6.cloned.1.call-done), kind=kOutput, calls=%fused_computation.81 | convolution fusion | flops 3221749760 | bytes 10485760 | tf_op jit(solution)/shard_map/tf,fjc->tjc/dot_general | solution.py:91
  83.9 2.0 copy-done.1
  86.0 1.6 fusion.43
  87.9 4.8 %fusion.21 = bf16[4,256,1024]{2,1,0:T(8,128)(2,1)} fusion(s32[]{:T(128)S(6)} %select_n.27, bf16[1,256,1024]{2,1,0:T(8,128)(2,1)S(1)} %bitcast.127, bf16[1,256,1024]{2,1,0:T(8,128)(2,1)S(1)} %bitcast.144, bf16[1,256,1024]{2,1,0:T(8,128)(2,1)} %bitcast.5, bf16[1,256,1024]{2,1,0:T(8,128)(2,1)} %bitcast.6), kind=kLoop, calls=%fused_computation.45 | loop fusion | flops 7340032 | bytes 4194308 | tf_op jit(solution)/shard_map/jit(_roll_dynamic)/concatenate | solution.py:32
  93.6 13.3 %all-gather.1 = f32[8,2,512]{2,1,0:T(2,128)S(1)} all-gather(f32[2,2,512]{2,1,0:T(2,128)S(1)} %pad_maximum_fusion.1), channel_id=3, replica_groups=mesh['groups'=2,'picks'=4,'heads'=4] {'picks'}, dimensions={0}, use_global_device_ids=true | all-gather | bytes 40960 | tf_op jit(solution)/shard_map/all_gather | solution.py:105
  106.9 7.8 %all-gather.10.cloned.1.call-done = bf16[8,512,128]{2,1,0:T(8,128)(2,1)} async-done(((bf16[2,512,128]{2,1,0:T(8,128)(2,1)}), bf16[8,512,128]{2,1,0:T(8,128)(2,1)}) %all-gather.10.cloned.1.call-update) | async-done | bytes 1048592 | tf_op jit(solution)/shard_map/all_gather | solution.py:104
  114.7 1.8 multiply_reduce_fusion.2
  118.6 5.6 %collective-permute-done.6 = bf16[256,512]{1,0:T(8,128)(2,1)S(1)} collective-permute-done((bf16[256,512]{1,0:T(8,128)(2,1)S(1)}, bf16[256,512]{1,0:T(8,128)(2,1)S(1)}, u32[]{:S(2)}, u32[]{:S(2)}) %collective-permute-start.6) | collective-permute-done | bytes 262176 | tf_op jit(solution)/shard_map/ppermute | solution.py:30
  124.2 6.7 %collective-permute-done.7 = bf16[256,512]{1,0:T(8,128)(2,1)S(1)} collective-permute-done((bf16[256,512]{1,0:T(8,128)(2,1)S(1)}, bf16[256,512]{1,0:T(8,128)(2,1)S(1)}, u32[]{:S(2)}, u32[]{:S(2)}) %collective-permute-start.7) | collective-permute-done | bytes 262176 | tf_op jit(solution)/shard_map/ppermute | solution.py:30
  131.1 2.2 %fusion.60 = bf16[4,256,512]{2,1,0:T(8,128)(2,1)S(1)} fusion(s32[]{:T(128)S(6)} %select_n.27, bf16[1,256,512]{2,1,0:T(8,128)(2,1)S(1)} %bitcast.133, bf16[1,256,512]{2,1,0:T(8,128)(2,1)S(1)} %bitcast.147, bf16[1,256,512]{2,1,0:T(8,128)(2,1)S(1)} %bitcast.148, bf16[1,256,512]{2,1,0:T(8,128)(2,1)} %bitcast.32), kind=kLoop, calls=%fused_computation.103 | loop fusion | flops 3670016 | bytes 2097156 | tf_op jit(solution)/shard_map/jit(_roll_dynamic)/concatenate | solution.py:32
  133.4 1.4 multiply_reduce_fusion.4
  137.1 1.5 collective-permute-start.10
  138.9 4.0 %collective-permute-done.9 = bf16[256,512]{1,0:T(8,128)(2,1)S(1)} collective-permute-done((bf16[256,512]{1,0:T(8,128)(2,1)S(1)}, bf16[256,512]{1,0:T(8,128)(2,1)S(1)}, u32[]{:S(2)}, u32[]{:S(2)}) %collective-permute-start.9) | collective-permute-done | bytes 262176 | tf_op jit(solution)/shard_map/ppermute | solution.py:30
  142.9 8.3 %collective-permute-done.10 = bf16[256,512]{1,0:T(8,128)(2,1)S(1)} collective-permute-done((bf16[256,512]{1,0:T(8,128)(2,1)S(1)}, bf16[256,512]{1,0:T(8,128)(2,1)S(1)}, u32[]{:S(2)}, u32[]{:S(2)}) %collective-permute-start.10) | collective-permute-done | bytes 262176 | tf_op jit(solution)/shard_map/ppermute | solution.py:30
  152.6 1.4 multiply_reduce_fusion.3
  154.0 1.3 copy-done.4
  156.3 5.1 %convolution_convert_fusion.2 = bf16[1024,256]{0,1:T(8,128)(2,1)S(1)} fusion(bf16[3072,1024]{1,0:T(8,128)(2,1)} %bitcast.119, bf16[3072,256]{1,0:T(8,128)(2,1)} %all-gather.8.cloned.1.call-done), kind=kOutput, calls=%fused_computation.84 | convolution fusion | flops 1610874880 | bytes 8388608 | tf_op jit(solution)/shard_map/dot_general | solution.py:153
  166.1 1.9 collective-permute-done.13
  168.6 1.2 multiply_convert_fusion.4
  170.2 3.1 %convolution_convert_fusion = bf16[3072,256]{1,0:T(8,128)(2,1)} fusion(bf16[3072,1024]{1,0:T(8,128)(2,1)S(1)} %bitcast.122, bf16[1024,256]{0,1:T(8,128)(2,1)S(1)} %bitcast.168), kind=kOutput, calls=%fused_computation.26 | convolution fusion | flops 1611399168 | bytes 8388608 | tf_op jit(solution)/shard_map/dot_general | solution.py:179
  173.4 1.9 constant_dynamic-slice_fusion
  175.2 32.4 %reduce-scatter.2.cloned.1.call-done = bf16[768,256]{1,0:T(8,128)(2,1)} async-done(((bf16[3072,256]{1,0:T(8,128)(2,1)}), bf16[768,256]{1,0:T(8,128)(2,1)}) %reduce-scatter.2.cloned.1.call-update) | async-done | bytes 393232 | tf_op jit(solution)/shard_map/reduce_scatter | solution.py:178
  207.6 1.9 convert_element_type.100
  (88 shorter events, 18.9 us)
Async XLA Ops:
  7.2 127.6 %copy-start = (bf16[3,1024,256]{2,1,0:T(8,128)(2,1)S(1)}, bf16[3,1024,256]{2,1,0:T(8,128)(2,1)}, u32[]{:S(2)}) copy-start(bf16[3,1024,256]{2,1,0:T(8,128)(2,1)} %param.23) | copy-start | bytes 4718596
  7.2 8.1 %copy-start.9 = (f32[3,1024]{1,0:T(4,128)S(1)}, f32[3,1024]{1,0:T(4,128)}, u32[]{:S(2)}) copy-start(f32[3,1024]{1,0:T(4,128)} %param.16) | copy-start | bytes 36868
  7.2 68.7 %all-gather.6.cloned.1.call-start = ((), (), s32[]{:S(2)}) async-start(), calls=%async_computation.1 | async-start | bytes 3932160 | tf_op jit(solution)/shard_map/all_gather | solution.py:89
  7.9 106.8 %all-gather.10.cloned.1.call-start = ((), (), s32[]{:S(2)}) async-start(), calls=%async_computation.4 | async-start | bytes 1310720 | tf_op jit(solution)/shard_map/all_gather | solution.py:104
  9.2 78.6 %collective-permute-start = (bf16[256,1024]{1,0:T(8,128)(2,1)S(1)}, bf16[256,1024]{1,0:T(8,128)(2,1)S(1)}, u32[]{:S(2)}, u32[]{:S(2)}) collective-permute-start(bf16[256,1024]{1,0:T(8,128)(2,1)S(1)} %bitcast.124), channel_id=1, source_target_pairs={{0,3},{1,0},{2,1},{3,2},{4,7},{5,4},{6,5},{7,6},{8,11},{9,8},{10,9... | collective-permute-start | bytes 1572872 | tf_op jit(solution)/shard_map/ppermute | solution.py:30
  11.7 76.2 %collective-permute-start.1 = (bf16[256,1024]{1,0:T(8,128)(2,1)S(1)}, bf16[256,1024]{1,0:T(8,128)(2,1)}, u32[]{:S(2)}, u32[]{:S(2)}) collective-permute-start(bf16[256,1024]{1,0:T(8,128)(2,1)S(1)} %bitcast.125), channel_id=1, source_target_pairs={{0,2},{1,3},{2,0},{3,1},{4,6},{5,7},{6,4},{7,5},{8,10},{9,11},{10,... | collective-permute-start | bytes 1572872 | tf_op jit(solution)/shard_map/ppermute | solution.py:30
  12.3 34.1 %collective-permute-start.3 = (bf16[256,1024]{1,0:T(8,128)(2,1)}, bf16[256,1024]{1,0:T(8,128)(2,1)}, u32[]{:S(2)}, u32[]{:S(2)}) collective-permute-start(bf16[256,1024]{1,0:T(8,128)(2,1)} %param.21), channel_id=1, source_target_pairs={{0,3},{1,0},{2,1},{3,2},{4,7},{5,4},{6,5},{7,6},{8,11},{9,8},{10,9... | collective-permute-start | bytes 1572872 | tf_op jit(solution)/shard_map/ppermute | solution.py:30
  12.4 43.9 %collective-permute-start.4 = (bf16[256,1024]{1,0:T(8,128)(2,1)}, bf16[256,1024]{1,0:T(8,128)(2,1)}, u32[]{:S(2)}, u32[]{:S(2)}) collective-permute-start(bf16[256,1024]{1,0:T(8,128)(2,1)} %param.21), channel_id=1, source_target_pairs={{0,2},{1,3},{2,0},{3,1},{4,6},{5,7},{6,4},{7,5},{8,10},{9,11},{10,... | collective-permute-start | bytes 1572872 | tf_op jit(solution)/shard_map/ppermute | solution.py:30
  14.1 42.2 %collective-permute-start.5 = (bf16[256,1024]{1,0:T(8,128)(2,1)}, bf16[256,1024]{1,0:T(8,128)(2,1)}, u32[]{:S(2)}, u32[]{:S(2)}) collective-permute-start(bf16[256,1024]{1,0:T(8,128)(2,1)} %param.21), channel_id=1, source_target_pairs={{0,1},{1,2},{2,3},{3,0},{4,5},{5,6},{6,7},{7,4},{8,9},{9,10},{10,1... | collective-permute-start | bytes 1572872 | tf_op jit(solution)/shard_map/ppermute | solution.py:30
  38.2 18.1 %copy-start.8 = (bf16[256,1024]{1,0:T(8,128)(2,1)S(1)}, bf16[256,1024]{1,0:T(8,128)(2,1)}, u32[]{:S(2)}) copy-start(bf16[256,1024]{1,0:T(8,128)(2,1)} %param.21) | copy-start | bytes 1572868
  46.4 41.4 %collective-permute-start.2 = (bf16[256,1024]{1,0:T(8,128)(2,1)S(1)}, bf16[256,1024]{1,0:T(8,128)(2,1)}, u32[]{:S(2)}, u32[]{:S(2)}) collective-permute-start(bf16[256,1024]{1,0:T(8,128)(2,1)S(1)} %bitcast.126), channel_id=1, source_target_pairs={{0,1},{1,2},{2,3},{3,0},{4,5},{5,6},{6,7},{7,4},{8,9},{9,10},{10,1... | collective-permute-start | bytes 1572872 | tf_op jit(solution)/shard_map/ppermute | solution.py:30
  83.9 2.0 copy-start.1
  87.6 68.7 %all-gather.8.cloned.1.call-start = ((), (), s32[]{:S(2)}) async-start(), calls=%async_computation.2 | async-start | bytes 1966080 | tf_op jit(solution)/shard_map/all_gather | solution.py:121
  87.8 4.8 %copy-start.2 = (f32[2,512,1024]{2,1,0:T(8,128)S(1)}, f32[2,512,1024]{2,1,0:T(8,128)}, u32[]{:S(2)}) copy-start(f32[2,512,1024]{2,1,0:T(8,128)} %copy-done.1) | copy-start | bytes 12582916
  93.5 24.9 %copy-start.10 = (f32[2,1024]{1,0:T(2,128)S(1)}, f32[2,1024]{1,0:T(2,128)}, u32[]{:S(2)}) copy-start(f32[2,1024]{1,0:T(2,128)} %param.22) | copy-start | bytes 24580
  116.7 16.7 %copy-start.6 = (bf16[512,1024]{1,0:T(8,128)(2,1)S(1)}, bf16[512,1024]{1,0:T(8,128)(2,1)}, u32[]{:S(2)}) copy-start(bf16[512,1024]{1,0:T(8,128)(2,1)} %param.19) | copy-start | bytes 3145732
  116.7 7.5 %collective-permute-start.6 = (bf16[256,512]{1,0:T(8,128)(2,1)S(1)}, bf16[256,512]{1,0:T(8,128)(2,1)S(1)}, u32[]{:S(2)}, u32[]{:S(2)}) collective-permute-start(bf16[256,512]{1,0:T(8,128)(2,1)S(1)} %bitcast.130), channel_id=1, source_target_pairs={{0,3},{1,0},{2,1},{3,2},{4,7},{5,4},{6,5},{7,6},{8,11},{9,8},{10,9... | collective-permute-start | bytes 786440 | tf_op jit(solution)/shard_map/ppermute | solution.py:30
  117.6 13.3 %collective-permute-start.7 = (bf16[256,512]{1,0:T(8,128)(2,1)S(1)}, bf16[256,512]{1,0:T(8,128)(2,1)S(1)}, u32[]{:S(2)}, u32[]{:S(2)}) collective-permute-start(bf16[256,512]{1,0:T(8,128)(2,1)S(1)} %bitcast.131), channel_id=1, source_target_pairs={{0,2},{1,3},{2,0},{3,1},{4,6},{5,7},{6,4},{7,5},{8,10},{9,11},{10,... | collective-permute-start | bytes 786440 | tf_op jit(solution)/shard_map/ppermute | solution.py:30
  118.3 12.8 %collective-permute-start.8 = (bf16[256,512]{1,0:T(8,128)(2,1)S(1)}, bf16[256,512]{1,0:T(8,128)(2,1)}, u32[]{:S(2)}, u32[]{:S(2)}) collective-permute-start(bf16[256,512]{1,0:T(8,128)(2,1)S(1)} %bitcast.132), channel_id=1, source_target_pairs={{0,1},{1,2},{2,3},{3,0},{4,5},{5,6},{6,7},{7,4},{8,9},{9,10},{10,1... | collective-permute-start | bytes 786440 | tf_op jit(solution)/shard_map/ppermute | solution.py:30
  118.5 89.1 %reduce-scatter.2.cloned.1.call-start = ((), (), s32[]{:S(2)}) async-start(), calls=%async_computation.3 | async-start | bytes 1966080 | tf_op jit(solution)/shard_map/reduce_scatter | solution.py:178
  118.6 14.8 %copy-start.3 = (bf16[4,256,1024]{2,1,0:T(8,128)(2,1)S(1)}, bf16[4,256,1024]{2,1,0:T(8,128)(2,1)}, u32[]{:S(2)}) copy-start(bf16[4,256,1024]{2,1,0:T(8,128)(2,1)} %fusion.14) | copy-start | bytes 6291460
  136.5 2.3 %copy-start.11 = (s32[1024]{0:T(1024)S(1)}, s32[1024]{0:T(1024)}, u32[]{:S(2)}) copy-start(s32[1024]{0:T(1024)} %param.17) | copy-start | bytes 12292
  136.5 2.3 %copy-start.13 = (f32[64]{0:T(128)S(1)}, f32[64]{0:T(128)}, u32[]{:S(2)}) copy-start(f32[64]{0:T(128)} %param.18) | copy-start | bytes 772
  137.1 15.5 %copy-start.5 = (bf16[4,256,1024]{2,1,0:T(8,128)(2,1)S(1)}, bf16[4,256,1024]{2,1,0:T(8,128)(2,1)}, u32[]{:S(2)}) copy-start(bf16[4,256,1024]{2,1,0:T(8,128)(2,1)} %fusion.21) | copy-start | bytes 6291460
  137.1 5.8 %collective-permute-start.9 = (bf16[256,512]{1,0:T(8,128)(2,1)S(1)}, bf16[256,512]{1,0:T(8,128)(2,1)S(1)}, u32[]{:S(2)}, u32[]{:S(2)}) collective-permute-start(bf16[256,512]{1,0:T(8,128)(2,1)S(1)} %bitcast.149), channel_id=1, source_target_pairs={{0,3},{1,0},{2,1},{3,2},{4,7},{5,4},{6,5},{7,6},{8,11},{9,8},{10,9... | collective-permute-start | bytes 786440 | tf_op jit(solution)/shard_map/ppermute | solution.py:30
  137.1 14.0 %collective-permute-start.10 = (bf16[256,512]{1,0:T(8,128)(2,1)S(1)}, bf16[256,512]{1,0:T(8,128)(2,1)S(1)}, u32[]{:S(2)}, u32[]{:S(2)}) collective-permute-start(bf16[256,512]{1,0:T(8,128)(2,1)S(1)} %bitcast.150), channel_id=1, source_target_pairs={{0,2},{1,3},{2,0},{3,1},{4,6},{5,7},{6,4},{7,5},{8,10},{9,11},{10,... | collective-permute-start | bytes 786440 | tf_op jit(solution)/shard_map/ppermute | solution.py:30
  138.6 12.7 %collective-permute-start.11 = (bf16[256,512]{1,0:T(8,128)(2,1)S(1)}, bf16[256,512]{1,0:T(8,128)(2,1)S(1)}, u32[]{:S(2)}, u32[]{:S(2)}) collective-permute-start(bf16[256,512]{1,0:T(8,128)(2,1)S(1)} %bitcast.151), channel_id=1, source_target_pairs={{0,1},{1,2},{2,3},{3,0},{4,5},{5,6},{6,7},{7,4},{8,9},{9,10},{10,1... | collective-permute-start | bytes 786440 | tf_op jit(solution)/shard_map/ppermute | solution.py:30
  152.6 2.8 %copy-start.7 = (bf16[2,1024,256]{2,1,0:T(8,128)(2,1)S(1)}, bf16[2,1024,256]{2,1,0:T(8,128)(2,1)}, u32[]{:S(2)}) copy-start(bf16[2,1024,256]{2,1,0:T(8,128)(2,1)} %param.25) | copy-start | bytes 3145732
  163.2 1.2 collective-permute-start.12
  164.4 3.6 %collective-permute-start.13 = (f32[1024]{0:T(1024)S(1)}, f32[1024]{0:T(1024)S(1)}, u32[]{:S(2)}, u32[]{:S(2)}) collective-permute-start(f32[1024]{0:T(1024)S(1)} %add.61), channel_id=1, source_target_pairs={{0,2},{1,3},{2,0},{3,1},{4,6},{5,7},{6,4},{7,5},{8,10},{9,11},{10,... | collective-permute-start | bytes 12296 | tf_op jit(solution)/shard_map/ppermute | solution.py:58
  165.3 4.6 %slice-start = ((s8[6291456]{0:T(1024)(128)(4,1)}), s8[4194304]{0:T(1024)(128)(4,1)S(1)}, s32[]{:S(2)}) async-start(s8[6291456]{0:T(1024)(128)(4,1)} %bitcast.120), calls=%async_computation.5 | async-start | bytes 8388608
  168.6 1.6 slice-start.1
  (2 other events, 2.2 us)
Sparse Core Ops, SparseCore 0:
  9.6 66.2 all-gather.5
  87.7 26.9 all-gather.9
  118.7 36.9 all-gather.7
  173.5 34.0 reduce-scatter.1
where the time goes:
time: 216 us
  waiting for transfers between devices  97 us (45%)
  other arithmetic  45.7 us (21%)
  matrix products  26.8 us (12%)
  between operations  14.2 us (7%)
  blocking collectives  13.3 us (6%)
  starting transfers between devices  10.7 us (5%)
  local copies, waits for them, and re-layouts  8.39 us (4%)
    ppermute x12, waiting for transfers between devices, ring_gather(): blocks.append(lax.ppermute(x, axis, [(i, (i - s) % n) for i in range(n)]))  38.8 us
    reduce_scatter x1, waiting for transfers between devices, on_device(): lax.psum_scatter(jnp.dot(enc.T, dquery, preferred_element_type=jnp.float3...  32.4 us
    another operation x1, other arithmetic  22.8 us
    all_gather x1, waiting for transfers between devices, on_device(): piece = lax.all_gather(kv_weight, 'picks', axis=0, tiled=True)  14.5 us
    concatenate x4, other arithmetic, ring_gather(): ordered = jnp.roll(flipped, idx, axis=0)  13.3 us
    all_gather x1, blocking collectives, on_device(): lax.all_gather(jnp.stack([top, total]), 'picks', axis=0, tiled=False)  13.3 us
    ppermute x12, starting transfers between devices, ring_gather(): blocks.append(lax.ppermute(x, axis, [(i, (i - s) % n) for i in range(n)]))  9.4 us
    all_gather x1, waiting for transfers between devices, on_device(): lax.all_gather(numer.astype(jnp.bfloat16), 'picks', axis=0, tiled=False)  7.77 us
  transfers between devices with their start and end apart: 18, of which 13 were waited for; matrix products, arithmetic and copies ran while one was open for 28% of the time, Pallas kernels for 0%

commit v1 on v0

--- a/solution.py
+++ b/solution.py
@@ -10,6 +10,28 @@
 PI = 3.141592653589793
 EPS = 1e-06
 RING_MAX = 4
+
+
+def laid_out(blocks, dim):
+    dims = list(blocks.shape[1:])
+    dims[dim] *= blocks.shape[0]
+    return jnp.moveaxis(blocks, 0, dim).reshape(dims)
+
+
+def collect(x, axis, dim):
+    size = lax.axis_size(axis)
+    pairs = [(i, (i + 1) % size) for i in range(size)]
+    back = [(b, a) for a, b in pairs]
+    lower, upper = ([], [])
+    for hop in range(size - 1):
+        if hop % 2 == 0:
+            lower.append(lax.ppermute(lower[-1] if lower else x, axis, pairs))
+        else:
+            upper.append(lax.ppermute(upper[-1] if upper else x, axis, back))
+    blocks = jnp.stack([*lower[::-1], x, *upper])
+    shift = lax.axis_index(axis) - len(lower)
+    blocks = blocks[(jnp.arange(size) - shift) % size]
+    return laid_out(blocks, dim)
 
 
 def encode(coords):
@@ -86,7 +108,7 @@
     column = lax.axis_index("heads") * local
     enc = encode(coords)
     cross_full = ring_gather(cross_out, "heads", n_heads)
-    piece = lax.all_gather(kv_weight, "picks", axis=0, tiled=True)
+    piece = collect(kv_weight, "picks", 0)
     cross_full, piece = lax.optimization_barrier((cross_full, piece))
     keys_vals = jnp.einsum("tf,fjc->tjc", enc, piece, preferred_element_type=jnp.float32).astype(
         jnp.bfloat16

time: 216 us -> 257 us (1.19)
  waiting for transfers between devices: 97 us -> 116 us
  local copies, waits for them, and re-layouts: 8.39 us -> 18.2 us
  other arithmetic: 45.7 us -> 52 us
  starting transfers between devices: 10.7 us -> 14.7 us
    ppermute x0 -> x3, waiting for transfers between devices: none -> 26.9 us  [the longest x2 17.3 us: collect(): lower.append(lax.ppermute(lower[-1] if lower else x, axis, pairs))]
    all_gather x1 -> x0, waiting for transfers between devices: 14.5 us -> none  [on_device(): piece = lax.all_gather(kv_weight, 'picks', axis=0, tiled=True)]
    gather x0 -> x1, local copies, waits for them, and re-layouts: none -> 9.81 us  [collect(): blocks = blocks[(jnp.arange(size) - shift) % size]]
    another operation x1 -> x2, other arithmetic: 22.8 us -> 29.4 us
    ppermute x0 -> x3, starting transfers between devices: none -> 5.12 us  [the longest x1 3.54 us: collect(): upper.append(lax.ppermute(upper[-1] if upper else x, axis, back))]
    ppermute x12, waiting for transfers between devices: 38.8 us -> 42.8 us  [ring_gather(): blocks.append(lax.ppermute(x, axis, [(i, (i - s) % n) for i in range(n)]))]
    all_gather x1, waiting for transfers between devices: 7.77 us -> 11.1 us  [on_device(): lax.all_gather(numer.astype(jnp.bfloat16), 'picks', axis=0, tiled=False)]
    concatenate x4 -> x3, other arithmetic: 13.3 us -> 10.8 us  [ring_gather(): ordered = jnp.roll(flipped, idx, axis=0)]
  transfers between devices with their start and end apart: 18 -> 20, of which waited for: 13 -> 14; matrix products, arithmetic and copies ran while one was open for 28% -> 20% of each run, Pallas kernels for 0% -> 0%
where the time goes in v1:
time: 257 us
  waiting for transfers between devices  116 us (45%)
  other arithmetic  52 us (20%)
  matrix products  28 us (11%)
  local copies, waits for them, and re-layouts  18.2 us (7%)
  starting transfers between devices  14.7 us (6%)
  between operations  14.2 us (6%)
  blocking collectives  13.5 us (5%)
    ppermute x12, waiting for transfers between devices, ring_gather(): blocks.append(lax.ppermute(x, axis, [(i, (i - s) % n) for i in range(n)]))  42.8 us
    reduce_scatter x1, waiting for transfers between devices, on_device(): lax.psum_scatter(jnp.dot(enc.T, dquery, preferred_element_type=jnp.float3...  32.4 us
    another operation x1, other arithmetic  22.8 us
    ppermute x2, waiting for transfers between devices, collect(): lower.append(lax.ppermute(lower[-1] if lower else x, axis, pairs))  17.3 us
    all_gather x1, blocking collectives, on_device(): lax.all_gather(jnp.stack([top, total]), 'picks', axis=0, tiled=False)  13.5 us
    all_gather x1, waiting for transfers between devices, on_device(): lax.all_gather(numer.astype(jnp.bfloat16), 'picks', axis=0, tiled=False)  11.1 us
    concatenate x3, other arithmetic, ring_gather(): ordered = jnp.roll(flipped, idx, axis=0)  10.8 us
    gather x1, local copies, waits for them, and re-layouts, collect(): blocks = blocks[(jnp.arange(size) - shift) % size]  9.81 us
  transfers between devices with their start and end apart: 20, of which 14 were waited for; matrix products, arithmetic and copies ran while one was open for 20% of the time, Pallas kernels for 0%

profile of v1, /device:TPU:0, one launch (start us, length us, event | category | flops | bytes accessed | tf_op | source)
XLA Modules:
  0.0 256.8 jit_solution(577362407669138862)
XLA Ops:
  7.2 2.4 collective-permute-start.3
  13.1 1.6 collective-permute-start.6
  15.9 6.2 %collective-permute-done.3 = bf16[256,1024]{1,0:T(8,128)(2,1)} collective-permute-done((bf16[256,1024]{1,0:T(8,128)(2,1)}, bf16[256,1024]{1,0:T(8,128)(2,1)}, u32[]{:S(2)}, u32[]{:S(2)}) %collective-permute-start.3) | collective-permute-done | bytes 524320 | tf_op jit(solution)/shard_map/ppermute | solution.py:52
  22.9 11.7 %collective-permute-done.4 = bf16[256,1024]{1,0:T(8,128)(2,1)} collective-permute-done((bf16[256,1024]{1,0:T(8,128)(2,1)}, bf16[256,1024]{1,0:T(8,128)(2,1)}, u32[]{:S(2)}, u32[]{:S(2)}) %collective-permute-start.4) | collective-permute-done | bytes 524320 | tf_op jit(solution)/shard_map/ppermute | solution.py:52
  34.6 22.8 %fusion = (bf16[3,512,1024]{2,1,0:T(8,128)(2,1)S(1)}, bf16[3,512,1024]{2,1,0:T(8,128)(2,1)S(1)}) fusion(f32[3,1024]{1,0:T(4,128)S(1)} %copy-done.9, f32[512]{0:T(512)S(1)} %maximum_multiply_fusion), kind=kLoop, calls=%fused_computation.3 | loop fusion | flops 4718592 | bytes 6305792 | tf_op jit(solution)/shard_map/convert
  57.4 3.2 %pad_maximum_fusion = bf16[6,512,1024]{2,1,0:T(8,128)(2,1)} fusion(bf16[3,512,1024]{2,1,0:T(8,128)(2,1)S(1)} %get-tuple-element.29, bf16[3,512,1024]{2,1,0:T(8,128)(2,1)S(1)} %get-tuple-element.28), kind=kLoop, calls=%fused_computation.5 | loop fusion | flops 3145728 | bytes 12582912 | tf_op jit(solution)/shard_map/concatenate | solution.py:40
  60.6 3.5 %collective-permute-start.8 = (bf16[768,2,256]{2,1,0:T(2,128)(2,1)S(1)}, bf16[768,2,256]{2,1,0:T(2,128)(2,1)S(1)}, u32[]{:S(2)}, u32[]{:S(2)}) collective-permute-start(bf16[768,2,256]{2,1,0:T(2,128)(2,1)S(1)} %copy-done.7), channel_id=1, source_target_pairs={{4,0},{8,4},{12,8},{0,12},{5,1},{9,5},{13,9},{1,13},{6,2},{10,6},{... | collective-permute-start | bytes 2359304 | tf_op jit(solution)/shard_map/ppermute | solution.py:30
  64.2 8.3 %fusion.14 = (bf16[4,256,1024]{2,1,0:T(8,128)(2,1)}, bf16[4,256,1024]{2,1,0:T(8,128)(2,1)}) fusion(s32[]{:T(128)S(6)} %select_n.52, bf16[1,256,1024]{2,1,0:T(8,128)(2,1)S(1)} %bitcast.155, bf16[1,256,1024]{2,1,0:T(8,128)(2,1)} %bitcast.13, bf16[1,256,1024]{2,1,0:T(8,128)(2,1)} %bitcast.14, bf16[1,256,1024]{2,1,0:T(8,128)(2,1)} %bitcast.15, ...), kind=kLoop, calls=%fused_computation.40 | loop fusion | flops 14680064 | bytes 8388612 | tf_op jit(solution)/shard_map/jit(_roll_dynamic)/concatenate | solution.py:54
  72.5 9.5 %collective-permute-done.8 = bf16[768,2,256]{2,1,0:T(2,128)(2,1)S(1)} collective-permute-done((bf16[768,2,256]{2,1,0:T(2,128)(2,1)S(1)}, bf16[768,2,256]{2,1,0:T(2,128)(2,1)S(1)}, u32[]{:S(2)}, u32[]{:S(2)}) %collective-permute-start.8) | collective-permute-done | bytes 786464 | tf_op jit(solution)/shard_map/ppermute | solution.py:30
  82.1 17.3 %collective-permute-done.7 = bf16[768,2,256]{2,1,0:T(2,128)(2,1)S(1)} collective-permute-done((bf16[768,2,256]{2,1,0:T(2,128)(2,1)S(1)}, bf16[768,2,256]{2,1,0:T(2,128)(2,1)S(1)}, u32[]{:S(2)}, u32[]{:S(2)}) %collective-permute-start.7) | collective-permute-done | bytes 786464 | tf_op jit(solution)/shard_map/ppermute | solution.py:28
  99.4 6.6 %pad_maximum_fusion.1 = bf16[4,768,2,256]{3,2,1,0:T(2,128)(2,1)} fusion(bf16[1,768,2,256]{3,2,1,0:T(2,128)(2,1)S(1)} %bitcast.153, bf16[1,768,2,256]{3,2,1,0:T(2,128)(2,1)S(1)} %bitcast.151, bf16[1,768,2,256]{3,2,1,0:T(2,128)(2,1)S(1)} %bitcast.152, bf16[1,768,2,256]{3,2,1,0:T(2,128)(2,1)S(1)} %bitcast.154), kind=kLoop, calls=%fused_computation.32 | loop fusion | flops 4718592 | bytes 6291456 | tf_op jit(solution)/shard_map/stack | solution.py:31
  106.0 9.8 %gather_fusion = bf16[4,768,2,256]{3,2,1,0:T(2,128)(2,1)} fusion(bf16[4,768,2,256]{3,2,1,0:T(2,128)(2,1)} %pad_maximum_fusion.1, s32[1024]{0:T(1024)S(1)} %pad_clamp_fusion), kind=kCustom, calls=%fused_computation | custom fusion | bytes 6291472 | tf_op jit(solution)/shard_map/gather | solution.py:33
  115.8 7.1 %fusion.32 = bf16[1024,2,256]{0,2,1:T(8,128)(2,1)S(1)} fusion(bf16[3072,1024,1]{1,0,2:T(8,128)(2,1)} %bitcast.125, bf16[3072,2,256]{2,1,0:T(2,128)(2,1)} %bitcast.131), kind=kOutput, calls=%fused_computation.83 | convolution fusion | flops 3221749760 | bytes 10485760 | tf_op jit(solution)/shard_map/tf,fjc->tjc/dot_general | solution.py:113
  123.9 2.1 copy-done.2
  126.0 1.6 fusion.43
  127.6 3.1 %fusion.4 = f32[2,512]{1,0:T(2,128)S(1)} fusion(f32[2,512,1024]{2,1,0:T(8,128)} %copy-done.2, f32[2,512]{1,0:T(2,128)S(1)} %get-tuple-element.32), kind=kLoop, calls=%fused_computation.30 | loop fusion | flops 3144704 | bytes 4202496 | tf_op jit(solution)/shard_map/reduce_sum | solution.py:122
  130.7 13.5 %all-gather.1 = f32[8,2,512]{2,1,0:T(2,128)S(1)} all-gather(f32[2,2,512]{2,1,0:T(2,128)S(1)} %pad_maximum_fusion.2), channel_id=3, replica_groups=mesh['groups'=2,'picks'=4,'heads'=4] {'picks'}, dimensions={0}, use_global_device_ids=true | all-gather | bytes 40960 | tf_op jit(solution)/shard_map/all_gather | solution.py:127
  144.2 11.1 %all-gather.7.cloned.1.call-done = bf16[8,512,128]{2,1,0:T(8,128)(2,1)} async-done(((bf16[2,512,128]{2,1,0:T(8,128)(2,1)}), bf16[8,512,128]{2,1,0:T(8,128)(2,1)}) %all-gather.7.cloned.1.call-update) | async-done | bytes 1048592 | tf_op jit(solution)/shard_map/all_gather | solution.py:126
  155.3 1.8 multiply_reduce_fusion.2
  159.2 5.4 %collective-permute-done.9 = bf16[256,512]{1,0:T(8,128)(2,1)S(1)} collective-permute-done((bf16[256,512]{1,0:T(8,128)(2,1)S(1)}, bf16[256,512]{1,0:T(8,128)(2,1)S(1)}, u32[]{:S(2)}, u32[]{:S(2)}) %collective-permute-start.9) | collective-permute-done | bytes 262176 | tf_op jit(solution)/shard_map/ppermute | solution.py:52
  164.6 6.9 %collective-permute-done.10 = bf16[256,512]{1,0:T(8,128)(2,1)S(1)} collective-permute-done((bf16[256,512]{1,0:T(8,128)(2,1)S(1)}, bf16[256,512]{1,0:T(8,128)(2,1)S(1)}, u32[]{:S(2)}, u32[]{:S(2)}) %collective-permute-start.10) | collective-permute-done | bytes 262176 | tf_op jit(solution)/shard_map/ppermute | solution.py:52
  172.9 2.6 %multiply_reduce_fusion.4 = (f32[512]{0:T(512)S(1)}, f32[512,1024]{1,0:T(8,128)S(1)}) fusion(bf16[1024,512]{1,0:T(8,128)(2,1)S(1)} %bitcast.130, bf16[1024,1024]{1,0:T(8,128)(2,1)S(1)} %bitcast.124, bf16[512,1024]{1,0:T(8,128)(2,1)} %param.19), kind=kOutput, calls=%fused_computation.77 | convolution fusion | flops 1075838464 | bytes 6293504 | tf_op jit(solution)/shard_map/dot_general | solution.py:145
  177.9 1.4 collective-permute-start.13
  179.6 4.2 %collective-permute-done.12 = bf16[256,512]{1,0:T(8,128)(2,1)S(1)} collective-permute-done((bf16[256,512]{1,0:T(8,128)(2,1)S(1)}, bf16[256,512]{1,0:T(8,128)(2,1)S(1)}, u32[]{:S(2)}, u32[]{:S(2)}) %collective-permute-start.12) | collective-permute-done | bytes 262176 | tf_op jit(solution)/shard_map/ppermute | solution.py:52
  183.7 8.0 %collective-permute-done.13 = bf16[256,512]{1,0:T(8,128)(2,1)S(1)} collective-permute-done((bf16[256,512]{1,0:T(8,128)(2,1)S(1)}, bf16[256,512]{1,0:T(8,128)(2,1)S(1)}, u32[]{:S(2)}, u32[]{:S(2)}) %collective-permute-start.13) | collective-permute-done | bytes 262176 | tf_op jit(solution)/shard_map/ppermute | solution.py:52
  193.2 1.4 multiply_reduce_fusion.3
  196.9 5.1 %convolution_convert_fusion.2 = bf16[1024,256]{0,1:T(8,128)(2,1)S(1)} fusion(bf16[3072,1024]{1,0:T(8,128)(2,1)} %bitcast.126, bf16[3072,256]{1,0:T(8,128)(2,1)} %all-gather.5.cloned.1.call-done), kind=kOutput, calls=%fused_computation.86 | convolution fusion | flops 1610874880 | bytes 8388608 | tf_op jit(solution)/shard_map/dot_general | solution.py:175
  206.6 2.0 collective-permute-done.16
  210.9 3.1 %convolution_convert_fusion = bf16[3072,256]{1,0:T(8,128)(2,1)} fusion(bf16[3072,1024]{1,0:T(8,128)(2,1)S(1)} %bitcast.129, bf16[1024,256]{0,1:T(8,128)(2,1)S(1)} %bitcast.180), kind=kOutput, calls=%fused_computation.27 | convolution fusion | flops 1611399168 | bytes 8388608 | tf_op jit(solution)/shard_map/dot_general | solution.py:201
  214.0 1.9 constant_dynamic-slice_fusion
  215.9 32.4 %reduce-scatter.2.cloned.1.call-done = bf16[768,256]{1,0:T(8,128)(2,1)} async-done(((bf16[3072,256]{1,0:T(8,128)(2,1)}), bf16[768,256]{1,0:T(8,128)(2,1)}) %reduce-scatter.2.cloned.1.call-update) | async-done | bytes 393232 | tf_op jit(solution)/shard_map/reduce_scatter | solution.py:200
  248.3 1.9 convert_element_type.100
  (94 shorter events, 23.0 us)
Async XLA Ops:
  7.2 168.3 %copy-start = (bf16[3,1024,256]{2,1,0:T(8,128)(2,1)S(1)}, bf16[3,1024,256]{2,1,0:T(8,128)(2,1)}, u32[]{:S(2)}) copy-start(bf16[3,1024,256]{2,1,0:T(8,128)(2,1)} %param.23) | copy-start | bytes 4718596
  7.2 27.4 %copy-start.9 = (f32[3,1024]{1,0:T(4,128)S(1)}, f32[3,1024]{1,0:T(4,128)}, u32[]{:S(2)}) copy-start(f32[3,1024]{1,0:T(4,128)} %param.16) | copy-start | bytes 36868
  7.2 148.1 %all-gather.7.cloned.1.call-start = ((), (), s32[]{:S(2)}) async-start(), calls=%async_computation.3 | async-start | bytes 1310720 | tf_op jit(solution)/shard_map/all_gather | solution.py:126
  7.2 14.9 %collective-permute-start.3 = (bf16[256,1024]{1,0:T(8,128)(2,1)}, bf16[256,1024]{1,0:T(8,128)(2,1)}, u32[]{:S(2)}, u32[]{:S(2)}) collective-permute-start(bf16[256,1024]{1,0:T(8,128)(2,1)} %param.21), channel_id=1, source_target_pairs={{0,3},{1,0},{2,1},{3,2},{4,7},{5,4},{6,5},{7,6},{8,11},{9,8},{10,9... | collective-permute-start | bytes 1572872 | tf_op jit(solution)/shard_map/ppermute | solution.py:52
  9.7 24.9 %collective-permute-start.4 = (bf16[256,1024]{1,0:T(8,128)(2,1)}, bf16[256,1024]{1,0:T(8,128)(2,1)}, u32[]{:S(2)}, u32[]{:S(2)}) collective-permute-start(bf16[256,1024]{1,0:T(8,128)(2,1)} %param.21), channel_id=1, source_target_pairs={{0,2},{1,3},{2,0},{3,1},{4,6},{5,7},{6,4},{7,5},{8,10},{9,11},{10,... | collective-permute-start | bytes 1572872 | tf_op jit(solution)/shard_map/ppermute | solution.py:52
  10.3 50.3 %collective-permute-start.5 = (bf16[256,1024]{1,0:T(8,128)(2,1)}, bf16[256,1024]{1,0:T(8,128)(2,1)}, u32[]{:S(2)}, u32[]{:S(2)}) collective-permute-start(bf16[256,1024]{1,0:T(8,128)(2,1)} %param.21), channel_id=1, source_target_pairs={{0,1},{1,2},{2,3},{3,0},{4,5},{5,6},{6,7},{7,4},{8,9},{9,10},{10,1... | collective-permute-start | bytes 1572872 | tf_op jit(solution)/shard_map/ppermute | solution.py:52
  11.7 52.5 %collective-permute-start.2 = (bf16[256,1024]{1,0:T(8,128)(2,1)S(1)}, bf16[256,1024]{1,0:T(8,128)(2,1)}, u32[]{:S(2)}, u32[]{:S(2)}) collective-permute-start(bf16[256,1024]{1,0:T(8,128)(2,1)S(1)} %bitcast.132), channel_id=1, source_target_pairs={{0,1},{1,2},{2,3},{3,0},{4,5},{5,6},{6,7},{7,4},{8,9},{9,10},{10,1... | collective-permute-start | bytes 1572872 | tf_op jit(solution)/shard_map/ppermute | solution.py:52
  13.1 51.1 %collective-permute-start.6 = (bf16[768,2,256]{2,1,0:T(2,128)(2,1)}, bf16[768,2,256]{2,1,0:T(2,128)(2,1)S(1)}, u32[]{:S(2)}, u32[]{:S(2)}) collective-permute-start(bf16[768,2,256]{2,1,0:T(2,128)(2,1)} %param.20), channel_id=1, source_target_pairs={{0,4},{4,8},{8,12},{12,0},{1,5},{5,9},{9,13},{13,1},{2,6},{6,10},{... | collective-permute-start | bytes 2359304 | tf_op jit(solution)/shard_map/ppermute | solution.py:28
  22.2 42.0 %collective-permute-start.1 = (bf16[256,1024]{1,0:T(8,128)(2,1)S(1)}, bf16[256,1024]{1,0:T(8,128)(2,1)}, u32[]{:S(2)}, u32[]{:S(2)}) collective-permute-start(bf16[256,1024]{1,0:T(8,128)(2,1)S(1)} %bitcast.133), channel_id=1, source_target_pairs={{0,2},{1,3},{2,0},{3,1},{4,6},{5,7},{6,4},{7,5},{8,10},{9,11},{10,... | collective-permute-start | bytes 1572872 | tf_op jit(solution)/shard_map/ppermute | solution.py:52
  34.6 29.6 %collective-permute-start = (bf16[256,1024]{1,0:T(8,128)(2,1)S(1)}, bf16[256,1024]{1,0:T(8,128)(2,1)}, u32[]{:S(2)}, u32[]{:S(2)}) collective-permute-start(bf16[256,1024]{1,0:T(8,128)(2,1)S(1)} %bitcast.134), channel_id=1, source_target_pairs={{0,3},{1,0},{2,1},{3,2},{4,7},{5,4},{6,5},{7,6},{8,11},{9,8},{10,9... | collective-permute-start | bytes 1572872 | tf_op jit(solution)/shard_map/ppermute | solution.py:52
  57.4 3.2 %copy-start.7 = (bf16[768,2,256]{2,1,0:T(2,128)(2,1)S(1)}, bf16[768,2,256]{2,1,0:T(2,128)(2,1)}, u32[]{:S(2)}) copy-start(bf16[768,2,256]{2,1,0:T(2,128)(2,1)} %param.20) | copy-start | bytes 2359300
  57.4 6.8 %copy-start.8 = (bf16[256,1024]{1,0:T(8,128)(2,1)S(1)}, bf16[256,1024]{1,0:T(8,128)(2,1)}, u32[]{:S(2)}) copy-start(bf16[256,1024]{1,0:T(8,128)(2,1)} %param.21) | copy-start | bytes 1572868
  60.6 21.4 %collective-permute-start.8 = (bf16[768,2,256]{2,1,0:T(2,128)(2,1)S(1)}, bf16[768,2,256]{2,1,0:T(2,128)(2,1)S(1)}, u32[]{:S(2)}, u32[]{:S(2)}) collective-permute-start(bf16[768,2,256]{2,1,0:T(2,128)(2,1)S(1)} %copy-done.7), channel_id=1, source_target_pairs={{4,0},{8,4},{12,8},{0,12},{5,1},{9,5},{13,9},{1,13},{6,2},{10,6},{... | collective-permute-start | bytes 2359304 | tf_op jit(solution)/shard_map/ppermute | solution.py:30
  64.2 35.2 %collective-permute-start.7 = (bf16[768,2,256]{2,1,0:T(2,128)(2,1)S(1)}, bf16[768,2,256]{2,1,0:T(2,128)(2,1)S(1)}, u32[]{:S(2)}, u32[]{:S(2)}) collective-permute-start(bf16[768,2,256]{2,1,0:T(2,128)(2,1)S(1)} %collective-permute-done.6), channel_id=1, source_target_pairs={{0,4},{4,8},{8,12},{12,0},{1,5},{5,9},{9,13},{13,1},{2,6},{6,10},{... | collective-permute-start | bytes 2359304 | tf_op jit(solution)/shard_map/ppermute | solution.py:28
  127.6 69.3 %all-gather.5.cloned.1.call-start = ((), (), s32[]{:S(2)}) async-start(), calls=%async_computation.1 | async-start | bytes 1966080 | tf_op jit(solution)/shard_map/all_gather | solution.py:143
  130.7 28.4 %copy-start.10 = (f32[2,1024]{1,0:T(2,128)S(1)}, f32[2,1024]{1,0:T(2,128)}, u32[]{:S(2)}) copy-start(f32[2,1024]{1,0:T(2,128)} %param.22) | copy-start | bytes 24580
  157.4 7.3 %collective-permute-start.9 = (bf16[256,512]{1,0:T(8,128)(2,1)S(1)}, bf16[256,512]{1,0:T(8,128)(2,1)S(1)}, u32[]{:S(2)}, u32[]{:S(2)}) collective-permute-start(bf16[256,512]{1,0:T(8,128)(2,1)S(1)} %bitcast.138), channel_id=1, source_target_pairs={{0,3},{1,0},{2,1},{3,2},{4,7},{5,4},{6,5},{7,6},{8,11},{9,8},{10,9... | collective-permute-start | bytes 786440 | tf_op jit(solution)/shard_map/ppermute | solution.py:52
  158.2 13.4 %collective-permute-start.10 = (bf16[256,512]{1,0:T(8,128)(2,1)S(1)}, bf16[256,512]{1,0:T(8,128)(2,1)S(1)}, u32[]{:S(2)}, u32[]{:S(2)}) collective-permute-start(bf16[256,512]{1,0:T(8,128)(2,1)S(1)} %bitcast.139), channel_id=1, source_target_pairs={{0,2},{1,3},{2,0},{3,1},{4,6},{5,7},{6,4},{7,5},{8,10},{9,11},{10,... | collective-permute-start | bytes 786440 | tf_op jit(solution)/shard_map/ppermute | solution.py:52
  159.0 12.7 %collective-permute-start.11 = (bf16[256,512]{1,0:T(8,128)(2,1)S(1)}, bf16[256,512]{1,0:T(8,128)(2,1)S(1)}, u32[]{:S(2)}, u32[]{:S(2)}) collective-permute-start(bf16[256,512]{1,0:T(8,128)(2,1)S(1)} %bitcast.140), channel_id=1, source_target_pairs={{0,1},{1,2},{2,3},{3,0},{4,5},{5,6},{6,7},{7,4},{8,9},{9,10},{10,1... | collective-permute-start | bytes 786440 | tf_op jit(solution)/shard_map/ppermute | solution.py:52
  159.2 89.2 %reduce-scatter.2.cloned.1.call-start = ((), (), s32[]{:S(2)}) async-start(), calls=%async_computation.2 | async-start | bytes 1966080 | tf_op jit(solution)/shard_map/reduce_scatter | solution.py:200
  159.2 13.7 %copy-start.3 = (bf16[4,256,1024]{2,1,0:T(8,128)(2,1)S(1)}, bf16[4,256,1024]{2,1,0:T(8,128)(2,1)}, u32[]{:S(2)}) copy-start(bf16[4,256,1024]{2,1,0:T(8,128)(2,1)} %get-tuple-element.42) | copy-start | bytes 6291460
  177.2 2.2 copy-start.11
  177.3 2.2 copy-start.13
  177.8 15.4 %copy-start.5 = (bf16[4,256,1024]{2,1,0:T(8,128)(2,1)S(1)}, bf16[4,256,1024]{2,1,0:T(8,128)(2,1)}, u32[]{:S(2)}) copy-start(bf16[4,256,1024]{2,1,0:T(8,128)(2,1)} %get-tuple-element.43) | copy-start | bytes 6291460
  177.8 5.9 %collective-permute-start.12 = (bf16[256,512]{1,0:T(8,128)(2,1)S(1)}, bf16[256,512]{1,0:T(8,128)(2,1)S(1)}, u32[]{:S(2)}, u32[]{:S(2)}) collective-permute-start(bf16[256,512]{1,0:T(8,128)(2,1)S(1)} %bitcast.160), channel_id=1, source_target_pairs={{0,3},{1,0},{2,1},{3,2},{4,7},{5,4},{6,5},{7,6},{8,11},{9,8},{10,9... | collective-permute-start | bytes 786440 | tf_op jit(solution)/shard_map/ppermute | solution.py:52
  177.9 13.8 %collective-permute-start.13 = (bf16[256,512]{1,0:T(8,128)(2,1)S(1)}, bf16[256,512]{1,0:T(8,128)(2,1)S(1)}, u32[]{:S(2)}, u32[]{:S(2)}) collective-permute-start(bf16[256,512]{1,0:T(8,128)(2,1)S(1)} %bitcast.161), channel_id=1, source_target_pairs={{0,2},{1,3},{2,0},{3,1},{4,6},{5,7},{6,4},{7,5},{8,10},{9,11},{10,... | collective-permute-start | bytes 786440 | tf_op jit(solution)/shard_map/ppermute | solution.py:52
  179.3 12.7 %collective-permute-start.14 = (bf16[256,512]{1,0:T(8,128)(2,1)S(1)}, bf16[256,512]{1,0:T(8,128)(2,1)S(1)}, u32[]{:S(2)}, u32[]{:S(2)}) collective-permute-start(bf16[256,512]{1,0:T(8,128)(2,1)S(1)} %bitcast.162), channel_id=1, source_target_pairs={{0,1},{1,2},{2,3},{3,0},{4,5},{5,6},{6,7},{7,4},{8,9},{9,10},{10,1... | collective-permute-start | bytes 786440 | tf_op jit(solution)/shard_map/ppermute | solution.py:52
  193.2 2.8 %copy-start.6 = (bf16[2,1024,256]{2,1,0:T(8,128)(2,1)S(1)}, bf16[2,1024,256]{2,1,0:T(8,128)(2,1)}, u32[]{:S(2)}) copy-start(bf16[2,1024,256]{2,1,0:T(8,128)(2,1)} %param.25) | copy-start | bytes 3145732
  203.8 1.2 collective-permute-start.15
  205.1 3.6 %collective-permute-start.16 = (f32[1024]{0:T(1024)S(1)}, f32[1024]{0:T(1024)S(1)}, u32[]{:S(2)}, u32[]{:S(2)}) collective-permute-start(f32[1024]{0:T(1024)S(1)} %add.87), channel_id=1, source_target_pairs={{0,2},{1,3},{2,0},{3,1},{4,6},{5,7},{6,4},{7,5},{8,10},{9,11},{10,... | collective-permute-start | bytes 12296 | tf_op jit(solution)/shard_map/ppermute | solution.py:80
  205.8 4.7 %slice-start = ((s8[6291456]{0:T(1024)(128)(4,1)}), s8[4194304]{0:T(1024)(128)(4,1)S(1)}, s32[]{:S(2)}) async-start(s8[6291456]{0:T(1024)(128)(4,1)} %bitcast.127), calls=%async_computation.4 | async-start | bytes 8388608
  210.9 39.4 %copy-start.1 = (bf16[3,1024,256]{2,1,0:T(8,128)(2,1)S(1)}, bf16[3,1024,256]{2,1,0:T(8,128)(2,1)}, u32[]{:S(2)}) copy-start(bf16[3,1024,256]{2,1,0:T(8,128)(2,1)} %param.23) | copy-start | bytes 4718596
  (4 other events, 5.9 us)
Sparse Core Ops, SparseCore 0:
  127.7 27.5 all-gather.6
  159.3 36.8 all-gather.4
  214.1 34.1 reduce-scatter.1
